TPU v7x, 32 devices: a whole 2x2x4 slice. The times are simulated.
32 devices in a mesh: dp: 8 (over z, y), tensor: 4 (over x, core).
Axes of the slice: x: 2, y: 2, z: 4, core: 2. Of those that a mesh axis runs over, the one named last changes fastest.
Arguments:
- up_inputs: bfloat16 [16384, 1024], P('dp'), may hold values from -6 to 6
- up_grad_out: bfloat16 [16384, 2816], P('dp', 'tensor'), may hold values from -0.125 to 0.125
- emb_ids: int32 [16384], P('dp'), may hold values from 0 to 4095
- emb_grad_out: bfloat16 [16384, 1024], P('dp', 'tensor'), may hold values from -6 to 6
- up_error: float32 [8, 1024, 2816], P('dp', None, 'tensor'), may hold values from -6 to 6
- emb_error: float32 [8, 4096, 1024], P('dp', None, 'tensor'), may hold values from -6 to 6
- up_moment: float32 [1024, 2816], P('dp', 'tensor'), may hold values from -2 to 2
- emb_moment: float32 [4096, 1024], P('dp', 'tensor'), may hold values from -2 to 2
- up_start: float32 [2816, 32], P('tensor'), may hold values from -0.109375 to 0.109375
- emb_start: float32 [1024, 32], P('tensor'), may hold values from -0.1875 to 0.1875
- up_gram_inv: float32 [2, 32, 32], replicated, may hold values from -2 to 3, as said below
- emb_gram_inv: float32 [2, 32, 32], replicated, may hold values from -2 to 3, as said below
- norm_grads: float32 [8, 2, 1024], P('dp'), may hold values from -6 to 6
- norm_moment: float32 [2, 1024], replicated, may hold values from -2 to 2
Outputs:
- up_error_new: float32 [8, 1024, 2816], P('dp', None, 'tensor')
- emb_error_new: float32 [8, 4096, 1024], P('dp', None, 'tensor')
- up_moment_new: float32 [1024, 2816], P('dp', 'tensor')
- emb_moment_new: float32 [4096, 1024], P('dp', 'tensor')
- up_step: bfloat16 [1024, 2816], P(None, 'tensor')
- emb_step: bfloat16 [4096, 1024], P(None, 'tensor')
- norm_moment_new: float32 [2, 1024], replicated
- norm_step: float32 [2, 1024], replicated
Inputs may be any that keep to these rules, and one draw needn't show every extreme that they name: `up_gram_inv`: inverse Gram factor of each power round. `emb_gram_inv`: inverse Gram factor of each power round.
All inputs are finite; a program needn't handle non-finite values.
Results may differ from a plain program's by a relative error of at most 0.001.
Values may be sent and summed in bfloat16 or wider, within the bound.
No kernel may reach another device: no remote copies, remote signals or barrier semaphores. Data moves between devices by JAX's collectives and lax.ppermute only.
A program may use at most 128 MiB of HBM per device.

v0:
```python
import math
import jax
import jax.numpy as jnp
from jax import lax
from jax.sharding import PartitionSpec as P

BETA = 0.9
HIGHEST = lax.Precision.HIGHEST


def normalized(left_sum, gram, rows):
    scale = lax.rsqrt(jnp.mean(left_sum * left_sum) + 1e-06) / math.sqrt(rows)
    return jnp.dot(left_sum, gram, precision=HIGHEST) * scale


def left_part(field, right):
    return jnp.dot(field, right, precision=HIGHEST)


def right_part(field, left):
    return lax.dot_general(field, left, (((0,), (0,)), ((), ())), precision=HIGHEST)


def outer(left, right):
    return lax.dot_general(left, right, (((1,), (1,)), ((), ())), precision=HIGHEST)


def sum_rights(up_field, emb_field, up_left, emb_left):
    return lax.psum((right_part(up_field, up_left), right_part(emb_field, emb_left)), "dp")


def per_device(
    up_inputs,
    up_grad_out,
    emb_ids,
    emb_grad_out,
    up_error,
    emb_error,
    up_moment,
    emb_moment,
    up_start,
    emb_start,
    up_gram_inv,
    emb_gram_inv,
    norm_grads,
    norm_moment,
):
    replicas = lax.axis_size("dp")
    up_field = (
        lax.dot_general(
            up_inputs, up_grad_out, (((0,), (0,)), ((), ())), preferred_element_type=jnp.float32
        )
        + up_error[0]
    )
    one_hot_rows = jax.nn.one_hot(emb_ids, emb_error.shape[1], dtype=jnp.bfloat16)
    emb_terms = lax.dot_general(
        one_hot_rows, emb_grad_out, (((0,), (0,)), ((), ())), preferred_element_type=jnp.float32
    )
    emb_field = emb_terms + emb_error[0]
    up_rows = up_field.shape[0]
    emb_rows = emb_field.shape[0]
    up_part = left_part(up_field, up_start)
    emb_part = left_part(emb_field, emb_start)
    up_sum, emb_sum = lax.psum((up_part, emb_part), ("dp", "tensor"))
    norm_total = lax.psum(norm_grads[0], "dp")
    up_left = normalized(up_sum, up_gram_inv[0], up_rows)
    emb_left = normalized(emb_sum, emb_gram_inv[0], emb_rows)
    up_right, emb_right = sum_rights(up_field, emb_field, up_left, emb_left)
    up_sum, emb_sum = lax.psum(
        (left_part(up_field, up_right), left_part(emb_field, emb_right)), ("dp", "tensor")
    )
    up_left = normalized(up_sum, up_gram_inv[1], up_rows)
    emb_left = normalized(emb_sum, emb_gram_inv[1], emb_rows)
    up_right, emb_right = sum_rights(up_field, emb_field, up_left, emb_left)
    up_approx = outer(up_left, up_right) / replicas
    emb_approx = outer(emb_left, emb_right) / replicas
    up_error_new = (up_field - up_approx)[None]
    emb_error_new = (emb_field - emb_approx)[None]
    up_count = up_moment.shape[0]
    emb_count = emb_moment.shape[0]
    position = lax.axis_index("dp")
    up_first = position * up_count
    emb_first = position * emb_count
    up_local = lax.dynamic_slice_in_dim(up_approx, up_first, up_count, 0)
    emb_local = lax.dynamic_slice_in_dim(emb_approx, emb_first, emb_count, 0)
    up_moment_new = BETA * up_moment + up_local
    emb_moment_new = BETA * emb_moment + emb_local
    up_piece = (up_local + BETA * up_moment_new).astype(jnp.bfloat16)
    emb_piece = (emb_local + BETA * emb_moment_new).astype(jnp.bfloat16)
    up_step, emb_step = (
        lax.all_gather(up_piece, "dp", axis=0, tiled=True),
        lax.all_gather(emb_piece, "dp", axis=0, tiled=True),
    )
    norm_mean = norm_total / replicas
    norm_moment_new = BETA * norm_moment + norm_mean
    norm_step = norm_mean + BETA * norm_moment_new
    return (
        up_error_new,
        emb_error_new,
        up_moment_new,
        emb_moment_new,
        up_step,
        emb_step,
        norm_moment_new,
        norm_step,
    )


def solution(mesh):
    return jax.shard_map(
        per_device,
        mesh=mesh,
        in_specs=(
            P("dp", None),
            P("dp", "tensor"),
            P("dp"),
            P("dp", "tensor"),
            P("dp", None, "tensor"),
            P("dp", None, "tensor"),
            P("dp", "tensor"),
            P("dp", "tensor"),
            P("tensor", None),
            P("tensor", None),
            P(),
            P(),
            P("dp", None, None),
            P(),
        ),
        out_specs=(
            P("dp", None, "tensor"),
            P("dp", None, "tensor"),
            P("dp", "tensor"),
            P("dp", "tensor"),
            P(None, "tensor"),
            P(None, "tensor"),
            P(),
            P(),
        ),
        check_vma=False,
    )
```

profile of v0, /device:TPU:0, one launch (start us, length us, event | category | flops | bytes accessed | tf_op | source)
XLA Modules:
  0.0 628.8 jit_solution(18083480141476725518)
XLA Ops:
  7.2 0.0 copy-start
  7.2 0.0 copy-start.12
  7.2 0.0 all-reduce.14.cloned.1.call-start
  7.2 11.9 %fusion.2 = f32[4096,256]{1,0:T(8,128)S(1)} fusion(bf16[2048,256]{1,0:T(8,128)(2,1)} %param.17, s32[2048]{0:T(1024)} %param.16, f32[1,4096,256]{2,1,0:T(8,128)} %param.19), kind=kOutput, calls=%fused_computation.4 | convolution fusion | flops 4304404480 | bytes 9445376 | tf_op jit(solution)/shard_map/dot_general | solution.py:56
  19.1 0.0 copy-done.12
  19.1 0.0 copy-start.1
  19.2 0.0 copy-start.18
  19.2 5.2 fusion.15
  24.4 0.0 copy-done
  24.4 0.0 copy-done.18
  24.4 5.0 bitcast_add_fusion
  29.4 0.0 copy-done.1
  29.4 0.0 copy-start.2
  29.4 1.6 copy-done.2
  30.9 0.0 copy-done.11
  30.9 2.5 fusion.11
  33.4 0.0 all-reduce.14.cloned.1.call-update
  33.5 0.0 all-reduce.8.cloned.1.call-start
  33.5 132.8 %all-reduce.14.cloned.1.call-done = (f32[1024,32]{0,1:T(8,128)}, f32[4096,32]{0,1:T(8,128)}) async-done(((f32[1024,32]{0,1:T(8,128)}, f32[4096,32]{0,1:T(8,128)}), (f32[1024,32]{0,1:T(8,128)}, f32[4096,32]{0,1:T(8,128)})) %all-reduce.14.cloned.1.call-update) | async-done | bytes 655376 | tf_op jit(solution)/shard_map/psum | solution.py:64
  166.3 1.8 multiply_reduce_fusion.1
  168.8 0.0 copy-done.13
  168.8 1.7 convolution_multiply_fusion.2
  170.5 8.5 %fusion.16 = f32[256,32]{1,0:T(8,128)S(1)} fusion(f32[4096,256]{1,0:T(8,128)} %copy-done.1, f32[4096,32]{0,1:T(8,128)S(1)} %convolution_multiply_fusion.2), kind=kOutput, calls=%fused_computation.36 | convolution fusion | flops 402653184 | bytes 4751360 | tf_op jit(solution)/shard_map/dot_general | solution.py:21
  179.0 37.7 %psum.68 = f32[256,32]{1,0:T(8,128)S(1)} all-reduce(f32[256,32]{1,0:T(8,128)S(1)} %fusion.16), channel_id=1, replica_groups=mesh['dp'=8,'tensor'=4] {'dp'}, use_global_device_ids=true, to_apply=%region_8.9 | all-reduce | flops 8192 | bytes 65536 | tf_op jit(solution)/shard_map/psum | solution.py:29
  216.7 0.6 multiply_reduce_fusion.3
  218.1 1.0 convolution_multiply_fusion.4
  219.1 5.0 fusion.12
  224.0 0.0 all-reduce.8.cloned.1.call-update
  224.0 0.0 all-reduce.12.cloned.1.call-start
  224.1 7.0 %fusion.17 = f32[4096,32]{0,1:T(8,128)} fusion(f32[4096,256]{1,0:T(8,128)} %copy-done.1, f32[256,32]{1,0:T(8,128)S(1)} %psum.68), kind=kOutput, calls=%fused_computation.37 | convolution fusion | flops 402653184 | bytes 4751360 | tf_op jit(solution)/shard_map/dot_general | solution.py:17
  231.1 61.0 %all-reduce.8.cloned.1.call-done = f32[704,32]{1,0:T(8,128)} async-done(((f32[704,32]{1,0:T(8,128)}), f32[704,32]{1,0:T(8,128)}) %all-reduce.8.cloned.1.call-update) | async-done | bytes 90128 | tf_op jit(solution)/shard_map/psum | solution.py:29
  292.0 4.3 fusion.13
  296.3 0.0 all-reduce.12.cloned.1.call-update
  296.4 0.0 all-reduce.10.cloned.1.call-start
  296.4 130.8 %all-reduce.12.cloned.1.call-done = (f32[1024,32]{0,1:T(8,128)}, f32[4096,32]{0,1:T(8,128)}) async-done(((f32[1024,32]{0,1:T(8,128)}, f32[4096,32]{0,1:T(8,128)}), (f32[1024,32]{0,1:T(8,128)}, f32[4096,32]{0,1:T(8,128)})) %all-reduce.12.cloned.1.call-update) | async-done | bytes 655376 | tf_op jit(solution)/shard_map/psum | solution.py:69
  427.2 1.5 multiply_reduce_fusion.2
  429.5 1.2 convolution_multiply_fusion.5
  430.7 5.0 fusion.14
  435.7 0.0 all-reduce.10.cloned.1.call-update
  435.7 0.3 all-gather.3.cloned.1.call-start
  436.0 70.5 %all-reduce.10.cloned.1.call-done = f32[704,32]{1,0:T(8,128)} async-done(((f32[704,32]{1,0:T(8,128)}), f32[704,32]{1,0:T(8,128)}) %all-reduce.10.cloned.1.call-update) | async-done | bytes 90128 | tf_op jit(solution)/shard_map/psum | solution.py:29
  506.5 3.4 convolution_multiply_fusion.3
  509.9 1.6 copy-done.5
  511.4 1.9 add_convert_fusion.1
  513.3 0.0 all-gather.3.cloned.1.call-update
  513.3 0.0 all-gather.5.cloned.1.call-start
  513.4 0.7 multiply_reduce_fusion
  514.8 1.7 convolution_multiply_fusion.1
  516.5 8.5 %fusion.18 = f32[256,32]{1,0:T(8,128)S(1)} fusion(f32[4096,256]{1,0:T(8,128)} %copy-done.1, f32[4096,32]{0,1:T(8,128)S(1)} %convolution_multiply_fusion.1), kind=kOutput, calls=%fused_computation.38 | convolution fusion | flops 402653184 | bytes 4751360 | tf_op jit(solution)/shard_map/dot_general | solution.py:21
  525.0 0.0 copy-start.16
  525.0 38.7 %all-reduce.2 = (f32[256,32]{1,0:T(8,128)}, f32[2,1024]{1,0:T(2,128)}) all-reduce(f32[256,32]{1,0:T(8,128)S(1)} %fusion.18, f32[2,1024]{1,0:T(2,128)S(1)} %bitcast.48), channel_id=1, replica_groups=mesh['dp'=8,'tensor'=4] {'dp'}, use_global_device_ids=true, to_apply=%region_11.12 | all-reduce | flops 10240 | bytes 81920 | tf_op jit(solution)/shard_map/psum | solution.py:29
  563.7 4.4 convolution_multiply_fusion
  568.2 0.0 copy-start.4
  568.2 1.9 copy-done.4
  570.1 1.0 add_convert_fusion
  571.1 0.0 all-gather.5.cloned.1.call-update
  571.1 0.0 copy-done.16
  571.1 0.0 copy-done.17
  571.1 0.6 multiply_add_fusion.2
  571.8 6.2 subtract_bitcast_fusion
  577.9 2.2 subtract_bitcast_fusion.1
  580.1 37.6 %all-gather.5.cloned.1.call-done = bf16[4096,256]{1,0:T(8,128)(2,1)} async-done(((bf16[512,256]{1,0:T(8,128)(2,1)}), bf16[4096,256]{1,0:T(8,128)(2,1)}) %all-gather.5.cloned.1.call-update) | async-done | bytes 2097168 | tf_op jit(solution)/shard_map/all_gather | solution.py:92
  617.7 2.7 copy.30
  620.4 1.3 copy.31
  (21 shorter events, 0.0 us)
Async XLA Ops:
  7.2 17.2 %copy-start = (bf16[2048,704]{0,1:T(8,128)(2,1)S(1)}, bf16[2048,704]{0,1:T(8,128)(2,1)}, u32[]{:S(2)}) copy-start(bf16[2048,704]{0,1:T(8,128)(2,1)} %param.15) | copy-start | bytes 8650756
  7.2 12.0 %copy-start.12 = (f32[256,32]{0,1:T(8,128)S(1)}, f32[256,32]{0,1:T(8,128)}, u32[]{:S(2)}) copy-start(f32[256,32]{0,1:T(8,128)} %param.23) | copy-start | bytes 98308
  7.2 159.1 %all-reduce.14.cloned.1.call-start = ((), (), s32[]{:S(2)}) async-start(), calls=%async_computation.5 | async-start | bytes 1310720 | tf_op jit(solution)/shard_map/psum | solution.py:64
  19.1 10.2 %copy-start.1 = (f32[4096,256]{1,0:T(8,128)}, f32[4096,256]{1,0:T(8,128)S(1)}, u32[]{:S(2)}) copy-start(f32[4096,256]{1,0:T(8,128)S(1)} %fusion.2) | copy-start | bytes 12582916
  19.2 5.2 copy-start.18
  24.4 6.6 %copy-start.11 = (f32[704,32]{0,1:T(8,128)S(1)}, f32[704,32]{0,1:T(8,128)}, u32[]{:S(2)}) copy-start(f32[704,32]{0,1:T(8,128)} %param.22) | copy-start | bytes 270340
  29.4 1.6 copy-start.2
  30.9 137.9 %copy-start.13 = (f32[2,32,32]{2,1,0:T(8,128)S(1)}, f32[2,32,32]{2,1,0:T(8,128)}, u32[]{:S(2)}) copy-start(f32[2,32,32]{2,1,0:T(8,128)} %param.25) | copy-start | bytes 24580
  33.4 184.6 %copy-start.14 = (f32[2,32,32]{2,1,0:T(8,128)S(1)}, f32[2,32,32]{2,1,0:T(8,128)}, u32[]{:S(2)}) copy-start(f32[2,32,32]{2,1,0:T(8,128)} %param.24) | copy-start | bytes 24580
  33.5 258.6 %all-reduce.8.cloned.1.call-start = ((), (), s32[]{:S(2)}) async-start(), calls=%async_computation | async-start | bytes 720896 | tf_op jit(solution)/shard_map/psum | solution.py:29
  166.3 50.4 %copy-start.9 = (f32[1024,32]{0,1:T(8,128)S(1)}, f32[1024,32]{0,1:T(8,128)}, u32[]{:S(2)}) copy-start(f32[1024,32]{0,1:T(8,128)} %get-tuple-element.10) | copy-start | bytes 393220
  224.0 203.2 %all-reduce.12.cloned.1.call-start = ((), (), s32[]{:S(2)}) async-start(), calls=%async_computation.4 | async-start | bytes 1310720 | tf_op jit(solution)/shard_map/psum | solution.py:69
  296.4 210.1 %all-reduce.10.cloned.1.call-start = ((), (), s32[]{:S(2)}) async-start(), calls=%async_computation.1 | async-start | bytes 720896 | tf_op jit(solution)/shard_map/psum | solution.py:29
  430.7 82.7 %copy-start.8 = (f32[4096,32]{0,1:T(8,128)S(1)}, f32[4096,32]{0,1:T(8,128)}, u32[]{:S(2)}) copy-start(f32[4096,32]{0,1:T(8,128)} %get-tuple-element.9) | copy-start | bytes 1572868
  435.7 144.4 %all-gather.3.cloned.1.call-start = ((), (), s32[]{:S(2)}) async-start(), calls=%async_computation.2 | async-start | bytes 1622016 | tf_op jit(solution)/shard_map/all_gather | solution.py:91
  509.8 1.6 copy-start.5
  511.4 13.5 %copy-start.15 = (f32[1,2,1024]{2,1,0:T(2,128)S(1)}, f32[1,2,1024]{2,1,0:T(2,128)}, u32[]{:S(2)}) copy-start(f32[1,2,1024]{2,1,0:T(2,128)} %param.26) | copy-start | bytes 24580
  513.3 104.4 %all-gather.5.cloned.1.call-start = ((), (), s32[]{:S(2)}) async-start(), calls=%async_computation.3 | async-start | bytes 2359296 | tf_op jit(solution)/shard_map/all_gather | solution.py:92
  525.0 46.2 %copy-start.16 = (f32[2,1024]{1,0:T(2,128)S(1)}, f32[2,1024]{1,0:T(2,128)}, u32[]{:S(2)}) copy-start(f32[2,1024]{1,0:T(2,128)} %param.27) | copy-start | bytes 24580
  563.7 6.4 %copy-start.10 = (f32[512,256]{1,0:T(8,128)S(1)}, f32[512,256]{1,0:T(8,128)}, u32[]{:S(2)}) copy-start(f32[512,256]{1,0:T(8,128)} %param.21) | copy-start | bytes 1572868
  563.7 7.4 %copy-start.17 = (f32[2,1024]{1,0:T(2,128)S(1)}, f32[2,1024]{1,0:T(2,128)}, u32[]{:S(2)}) copy-start(f32[2,1024]{1,0:T(2,128)} %get-tuple-element.13) | copy-start | bytes 24580
  568.2 2.0 copy-start.4
  571.8 6.2 copy-start.3
  571.8 6.2 copy-start.6
  617.7 2.7 copy-start.7
Sparse Core Ops, SparseCore 0:
  33.6 132.6 all-reduce.13
  224.2 67.8 all-reduce.7
  298.0 129.1 all-reduce.11
  435.8 70.5 all-reduce.9
  513.5 44.3 all-gather.2
  571.2 46.4 all-gather.4
where the time goes:
time: 638 us; the launch traced here: 629 us
  waiting for transfers between devices  433 us (68%)
  blocking collectives  76.5 us (12%)
  matrix products  76 us (12%)
  between operations  17.4 us (3%)
  other arithmetic  16.5 us (3%)
  local copies, waits for them, and re-layouts  9.22 us (1%)
    psum x1, waiting for transfers between devices, per_device(): up_sum, emb_sum = lax.psum((up_part, emb_part), ('dp', 'tensor'))  133 us
    psum x2, waiting for transfers between devices, sum_rights(): lax.psum((right_part(up_field, up_left), right_part(emb_field, emb_left))...  131 us
    psum x1, waiting for transfers between devices, per_device(): lax.psum((left_part(up_field, up_right), left_part(emb_field, emb_right))...  131 us
    psum x2, blocking collectives, sum_rights(): lax.psum((right_part(up_field, up_left), right_part(emb_field, emb_left))...  76.5 us
    all_gather x1, waiting for transfers between devices, per_device(): lax.all_gather(emb_piece, 'dp', axis=0, tiled=True)  37.6 us
    dot_general x4, matrix products, right_part(): lax.dot_general(field, left, (((0,), (0,)), ((), ())), precision=HIGHEST)  26.9 us
    dot_general x4, matrix products, left_part(): return jnp.dot(field, right, precision=HIGHEST)  18.9 us
  transfers between devices with their start and end apart: 6, of which 5 were waited for; matrix products, arithmetic and copies ran while one was open for 5% of the time, Pallas kernels for 0%

commit v1 on v0

--- a/solution.py
+++ b/solution.py
@@ -6,6 +6,27 @@
 
 BETA = 0.9
 HIGHEST = lax.Precision.HIGHEST
+
+
+def collect(array, axis, dim):
+    count, index, rows = (lax.axis_size(axis), lax.axis_index(axis), array.shape[dim])
+    ahead = [(i, (i + 1) % count) for i in range(count)]
+    behind = [(i, (i - 1) % count) for i in range(count)]
+    filled = jnp.zeros((*array.shape[:dim], count * rows, *array.shape[dim + 1 :]), array.dtype)
+    filled = lax.dynamic_update_slice_in_dim(filled, array, index * rows, axis=dim)
+    from_left = from_right = array
+    half = count // 2
+    for step in range(1, half + 1):
+        from_left = lax.ppermute(from_left, axis, ahead)
+        filled = lax.dynamic_update_slice_in_dim(
+            filled, from_left, (index - step) % count * rows, axis=dim
+        )
+        if step < count - half:
+            from_right = lax.ppermute(from_right, axis, behind)
+            filled = lax.dynamic_update_slice_in_dim(
+                filled, from_right, (index + step) % count * rows, axis=dim
+            )
+    return filled
 
 
 def normalized(left_sum, gram, rows):
@@ -89,7 +110,7 @@
     emb_piece = (emb_local + BETA * emb_moment_new).astype(jnp.bfloat16)
     up_step, emb_step = (
         lax.all_gather(up_piece, "dp", axis=0, tiled=True),
-        lax.all_gather(emb_piece, "dp", axis=0, tiled=True),
+        collect(emb_piece, "dp", 0),
     )
     norm_mean = norm_total / replicas
     norm_moment_new = BETA * norm_moment + norm_mean

time: 638 us -> 547 us (0.86)
  waiting for transfers between devices: 433 us -> 317 us
  starting transfers between devices: 0.46 us -> 16.9 us
  local copies, waits for them, and re-layouts: 9.22 us -> 19.1 us
    psum x2, waiting for transfers between devices: 131 us -> 22.5 us  [sum_rights(): lax.psum((right_part(up_field, up_left), right_part(emb_field, emb_left))...]
    all_gather x1 -> x0, waiting for transfers between devices: 37.6 us -> none  [per_device(): lax.all_gather(emb_piece, 'dp', axis=0, tiled=True)]
    ppermute x0 -> x7, waiting for transfers between devices: none -> 17.2 us  [the longest x4 17.2 us: collect(): from_left = lax.ppermute(from_left, axis, ahead)]
    ppermute x0 -> x7, starting transfers between devices: none -> 16.6 us  [the longest x3 10.6 us: collect(): from_right = lax.ppermute(from_right, axis, behind)]
    all_gather x1, waiting for transfers between devices: 0.01 us -> 14 us  [per_device(): lax.all_gather(up_piece, 'dp', axis=0, tiled=True)]
    dynamic_update_slice x0 -> x7, local copies, waits for them, and re-layouts: none -> 6.93 us  [the longest x4 3.83 us: collect(): lax.dynamic_update_slice_in_dim(filled, from_left, (index - step) % count...]
  transfers between devices with their start and end apart: 6 -> 12, of which waited for: 5 -> 8; matrix products, arithmetic and copies ran while one was open for 5% -> 10% of each run, Pallas kernels for 0% -> 0%
where the time goes in v1:
time: 547 us; the launch traced here: 538 us
  waiting for transfers between devices  317 us (58%)
  blocking collectives  76.8 us (14%)
  matrix products  75.3 us (14%)
  local copies, waits for them, and re-layouts  19.1 us (3%)
  between operations  17.1 us (3%)
  starting transfers between devices  16.9 us (3%)
  other arithmetic  15.6 us (3%)
    psum x1, waiting for transfers between devices, per_device(): up_sum, emb_sum = lax.psum((up_part, emb_part), ('dp', 'tensor'))  133 us
    psum x1, waiting for transfers between devices, per_device(): lax.psum((left_part(up_field, up_right), left_part(emb_field, emb_right))...  131 us
    psum x2, blocking collectives, sum_rights(): lax.psum((right_part(up_field, up_left), right_part(emb_field, emb_left))...  76.8 us
    dot_general x4, matrix products, right_part(): lax.dot_general(field, left, (((0,), (0,)), ((), ())), precision=HIGHEST)  27.5 us
    psum x2, waiting for transfers between devices, sum_rights(): lax.psum((right_part(up_field, up_left), right_part(emb_field, emb_left))...  22.5 us
    dot_general x4, matrix products, left_part(): return jnp.dot(field, right, precision=HIGHEST)  18.4 us
    ppermute x4, waiting for transfers between devices, collect(): from_left = lax.ppermute(from_left, axis, ahead)  17.2 us
    all_gather x1, waiting for transfers between devices, per_device(): lax.all_gather(up_piece, 'dp', axis=0, tiled=True)  14 us
  transfers between devices with their start and end apart: 12, of which 8 were waited for; matrix products, arithmetic and copies ran while one was open for 10% of the time, Pallas kernels for 0%

profile of v1, /device:TPU:0, one launch (start us, length us, event | category | flops | bytes accessed | tf_op | source)
XLA Modules:
  0.0 537.9 jit_solution(5984600271100244012)
XLA Ops:
  7.2 0.0 all-reduce.14.cloned.1.call-start
  7.2 1.7 copy-done
  9.0 6.4 %bitcast_add_fusion = f32[1024,704]{0,1:T(8,128)S(1)} fusion(f32[1,1024,704]{1,2,0:T(8,128)} %param.18, bf16[2048,704]{0,1:T(8,128)(2,1)S(1)} %copy-done, bf16[2048,1024]{1,0:T(8,128)(2,1)} %param.14), kind=kOutput, calls=%fused_computation.8 | convolution fusion | flops 2953510912 | bytes 12845056 | tf_op jit(solution)/shard_map/dot_general | solution.py:71
  15.4 1.6 copy-done.2
  16.9 2.5 fusion.11
  19.4 9.7 %fusion.2 = f32[4096,256]{1,0:T(8,128)S(1)} fusion(bf16[2048,256]{1,0:T(8,128)(2,1)S(1)} %copy-done.18, s32[2048]{0:T(1024)S(1)} %copy-done.19, f32[1,4096,256]{2,1,0:T(8,128)S(1)} %copy-done.17), kind=kOutput, calls=%fused_computation.4 | convolution fusion | flops 4304404480 | bytes 9445376 | tf_op jit(solution)/shard_map/dot_general | solution.py:77
  29.2 2.0 copy-done.1
  31.2 4.7 fusion.15
  35.9 0.0 all-reduce.14.cloned.1.call-update
  35.9 0.0 all-reduce.8.cloned.1.call-start
  36.0 132.7 %all-reduce.14.cloned.1.call-done = (f32[1024,32]{0,1:T(8,128)}, f32[4096,32]{0,1:T(8,128)}) async-done(((f32[1024,32]{0,1:T(8,128)}, f32[4096,32]{0,1:T(8,128)}), (f32[1024,32]{0,1:T(8,128)}, f32[4096,32]{0,1:T(8,128)})) %all-reduce.14.cloned.1.call-update) | async-done | bytes 655376 | tf_op jit(solution)/shard_map/psum | solution.py:85
  168.7 1.6 multiply_reduce_fusion.3
  171.0 1.9 convolution_multiply_fusion.4
  172.9 5.0 fusion.12
  177.9 0.0 all-reduce.8.cloned.1.call-update
  177.9 0.0 all-reduce.12.cloned.1.call-start
  178.0 0.7 multiply_reduce_fusion.1
  179.4 0.6 convolution_multiply_fusion.2
  180.0 8.5 %fusion.16 = f32[256,32]{1,0:T(8,128)S(1)} fusion(f32[4096,256]{1,0:T(8,128)} %copy-done.1, f32[4096,32]{0,1:T(8,128)S(1)} %convolution_multiply_fusion.2), kind=kOutput, calls=%fused_computation.44 | convolution fusion | flops 402653184 | bytes 4751360 | tf_op jit(solution)/shard_map/dot_general | solution.py:42
  188.5 37.5 %psum.68 = f32[256,32]{1,0:T(8,128)S(1)} all-reduce(f32[256,32]{1,0:T(8,128)S(1)} %fusion.16), channel_id=1, replica_groups=mesh['dp'=8,'tensor'=4] {'dp'}, use_global_device_ids=true, to_apply=%region_8.9 | all-reduce | flops 8192 | bytes 65536 | tf_op jit(solution)/shard_map/psum | solution.py:50
  226.1 6.9 %fusion.17 = f32[4096,32]{0,1:T(8,128)} fusion(f32[4096,256]{1,0:T(8,128)} %copy-done.1, f32[256,32]{1,0:T(8,128)S(1)} %psum.68), kind=kOutput, calls=%fused_computation.45 | convolution fusion | flops 402653184 | bytes 4751360 | tf_op jit(solution)/shard_map/dot_general | solution.py:38
  233.0 15.8 %all-reduce.8.cloned.1.call-done = f32[704,32]{1,0:T(8,128)} async-done(((f32[704,32]{1,0:T(8,128)}), f32[704,32]{1,0:T(8,128)}) %all-reduce.8.cloned.1.call-update) | async-done | bytes 90128 | tf_op jit(solution)/shard_map/psum | solution.py:50
  248.7 4.3 fusion.13
  253.0 0.0 all-reduce.12.cloned.1.call-update
  253.1 0.0 all-reduce.10.cloned.1.call-start
  253.2 130.8 %all-reduce.12.cloned.1.call-done = (f32[1024,32]{0,1:T(8,128)}, f32[4096,32]{0,1:T(8,128)}) async-done(((f32[1024,32]{0,1:T(8,128)}, f32[4096,32]{0,1:T(8,128)}), (f32[1024,32]{0,1:T(8,128)}, f32[4096,32]{0,1:T(8,128)})) %all-reduce.12.cloned.1.call-update) | async-done | bytes 655376 | tf_op jit(solution)/shard_map/psum | solution.py:90
  384.0 1.6 multiply_reduce_fusion.2
  386.3 1.2 convolution_multiply_fusion.5
  387.5 4.9 fusion.14
  392.5 0.0 all-gather.2.cloned.1.call-start
  392.6 0.7 multiply_reduce_fusion
  394.0 1.7 convolution_multiply_fusion.1
  395.7 9.2 %fusion.18 = f32[256,32]{1,0:T(8,128)} fusion(f32[4096,256]{1,0:T(8,128)} %copy-done.1, f32[4096,32]{0,1:T(8,128)S(1)} %convolution_multiply_fusion.1), kind=kOutput, calls=%fused_computation.46 | convolution fusion | flops 402653184 | bytes 4751360 | tf_op jit(solution)/shard_map/dot_general | solution.py:42
  404.8 39.2 %all-reduce.2 = (f32[256,32]{1,0:T(8,128)}, f32[2,1024]{1,0:T(2,128)S(1)}) all-reduce(f32[256,32]{1,0:T(8,128)} %fusion.18, f32[2,1024]{1,0:T(2,128)S(1)} %bitcast.48), channel_id=1, replica_groups=mesh['dp'=8,'tensor'=4] {'dp'}, use_global_device_ids=true, to_apply=%region_11.12 | all-reduce | flops 10240 | bytes 81920 | tf_op jit(solution)/shard_map/psum | solution.py:50
  444.1 4.5 convolution_multiply_fusion
  448.6 1.6 broadcast_in_dim.13
  450.2 1.0 copy-done.4
  451.2 1.1 constant_dynamic-update-slice_fusion.7
  452.3 4.7 collective-permute-start.1
  457.0 6.7 %all-reduce.10.cloned.1.call-done = f32[704,32]{1,0:T(8,128)} async-done(((f32[704,32]{1,0:T(8,128)}), f32[704,32]{1,0:T(8,128)}) %all-reduce.10.cloned.1.call-update) | async-done | bytes 90128 | tf_op jit(solution)/shard_map/psum | solution.py:50
  463.7 3.4 convolution_multiply_fusion.3
  467.1 1.6 copy-done.5
  468.7 0.9 add_convert_fusion.1
  469.5 0.0 all-gather.2.cloned.1.call-update
  469.6 6.2 %subtract_bitcast_fusion = f32[1,4096,256]{2,1,0:T(8,128)} fusion(f32[4096,256]{1,0:T(8,128)} %copy-done.1, f32[4096,256]{1,0:T(8,128)} %copy-done.4), kind=kLoop, calls=%fused_computation.7 | loop fusion | flops 1048576 | bytes 12582912 | tf_op jit(solution)/shard_map/broadcast_in_dim | solution.py:99
  475.8 0.6 multiply_add_fusion.2
  476.4 1.2 collective-permute-start.2
  477.6 3.5 collective-permute-start.3
  481.1 2.2 subtract_bitcast_fusion.1
  483.3 7.5 %collective-permute-done.2 = bf16[512,256]{1,0:T(8,128)(2,1)S(1)} collective-permute-done((bf16[512,256]{1,0:T(8,128)(2,1)}, bf16[512,256]{1,0:T(8,128)(2,1)S(1)}, u32[]{:S(2)}, u32[]{:S(2)}) %collective-permute-start.2) | collective-permute-done | bytes 262176 | tf_op jit(solution)/shard_map/ppermute | solution.py:20
  490.8 2.4 collective-permute-start.4
  493.1 1.7 constant_dynamic-update-slice_fusion.6
  494.8 1.7 constant_dynamic-update-slice_fusion.5
  496.5 2.3 collective-permute-start.5
  498.8 0.7 constant_dynamic-update-slice_fusion.4
  499.6 5.2 collective-permute-done.4
  504.7 2.5 collective-permute-start.6
  507.2 0.7 constant_dynamic-update-slice_fusion.3
  507.9 0.7 constant_dynamic-update-slice_fusion.2
  508.7 0.7 constant_dynamic-update-slice_fusion.1
  509.4 4.5 collective-permute-done.6
  513.9 0.7 constant_dynamic-update-slice_fusion
  514.6 14.0 %all-gather.2.cloned.1.call-done = bf16[1024,704]{0,1:T(8,128)(2,1)} async-done(((bf16[128,704]{0,1:T(8,128)(2,1)}), bf16[1024,704]{0,1:T(8,128)(2,1)}) %all-gather.2.cloned.1.call-update) | async-done | bytes 1441808 | tf_op jit(solution)/shard_map/all_gather | solution.py:112
  528.6 2.6 copy.37
  (41 shorter events, 0.1 us)
Async XLA Ops:
  7.2 1.8 copy-start
  7.2 9.8 %copy-start.11 = (f32[704,32]{0,1:T(8,128)S(1)}, f32[704,32]{0,1:T(8,128)}, u32[]{:S(2)}) copy-start(f32[704,32]{0,1:T(8,128)} %param.22) | copy-start | bytes 270340
  7.2 161.5 %all-reduce.14.cloned.1.call-start = ((), (), s32[]{:S(2)}) async-start(), calls=%async_computation.4 | async-start | bytes 1310720 | tf_op jit(solution)/shard_map/psum | solution.py:85
  9.0 10.4 %copy-start.17 = (f32[1,4096,256]{2,1,0:T(8,128)S(1)}, f32[1,4096,256]{2,1,0:T(8,128)}, u32[]{:S(2)}) copy-start(f32[1,4096,256]{2,1,0:T(8,128)} %param.19) | copy-start | bytes 12582916
  15.4 1.6 copy-start.2
  16.9 2.5 copy-start.18
  16.9 2.5 copy-start.19
  19.4 11.7 %copy-start.12 = (f32[256,32]{0,1:T(8,128)S(1)}, f32[256,32]{0,1:T(8,128)}, u32[]{:S(2)}) copy-start(f32[256,32]{0,1:T(8,128)} %param.23) | copy-start | bytes 98308
  29.1 2.0 copy-start.1
  31.2 139.8 %copy-start.14 = (f32[2,32,32]{2,1,0:T(8,128)S(1)}, f32[2,32,32]{2,1,0:T(8,128)}, u32[]{:S(2)}) copy-start(f32[2,32,32]{2,1,0:T(8,128)} %param.24) | copy-start | bytes 24580
  35.9 143.5 %copy-start.13 = (f32[2,32,32]{2,1,0:T(8,128)S(1)}, f32[2,32,32]{2,1,0:T(8,128)}, u32[]{:S(2)}) copy-start(f32[2,32,32]{2,1,0:T(8,128)} %param.25) | copy-start | bytes 24580
  35.9 212.8 %all-reduce.8.cloned.1.call-start = ((), (), s32[]{:S(2)}) async-start(), calls=%async_computation | async-start | bytes 720896 | tf_op jit(solution)/shard_map/psum | solution.py:50
  168.7 9.3 %copy-start.8 = (f32[4096,32]{0,1:T(8,128)S(1)}, f32[4096,32]{0,1:T(8,128)}, u32[]{:S(2)}) copy-start(f32[4096,32]{0,1:T(8,128)} %get-tuple-element.11) | copy-start | bytes 1572868
  177.9 206.1 %all-reduce.12.cloned.1.call-start = ((), (), s32[]{:S(2)}) async-start(), calls=%async_computation.3 | async-start | bytes 1310720 | tf_op jit(solution)/shard_map/psum | solution.py:90
  253.1 210.6 %all-reduce.10.cloned.1.call-start = ((), (), s32[]{:S(2)}) async-start(), calls=%async_computation.1 | async-start | bytes 720896 | tf_op jit(solution)/shard_map/psum | solution.py:50
  384.0 8.5 %copy-start.7 = (f32[4096,32]{0,1:T(8,128)S(1)}, f32[4096,32]{0,1:T(8,128)}, u32[]{:S(2)}) copy-start(f32[4096,32]{0,1:T(8,128)} %get-tuple-element.9) | copy-start | bytes 1572868
  392.5 136.1 %all-gather.2.cloned.1.call-start = ((), (), s32[]{:S(2)}) async-start(), calls=%async_computation.2 | async-start | bytes 1622016 | tf_op jit(solution)/shard_map/all_gather | solution.py:112
  394.0 10.8 %copy-start.15 = (f32[1,2,1024]{2,1,0:T(2,128)S(1)}, f32[1,2,1024]{2,1,0:T(2,128)}, u32[]{:S(2)}) copy-start(f32[1,2,1024]{2,1,0:T(2,128)} %param.26) | copy-start | bytes 24580
  444.1 7.1 %copy-start.9 = (f32[512,256]{1,0:T(8,128)S(1)}, f32[512,256]{1,0:T(8,128)}, u32[]{:S(2)}) copy-start(f32[512,256]{1,0:T(8,128)} %param.21) | copy-start | bytes 1572868
  448.6 2.6 copy-start.4
  451.2 17.5 %copy-start.10 = (f32[128,704]{0,1:T(8,128)S(1)}, f32[128,704]{0,1:T(8,128)}, u32[]{:S(2)}) copy-start(f32[128,704]{0,1:T(8,128)} %param.20) | copy-start | bytes 1081348
  452.2 24.1 %collective-permute-start = (bf16[512,256]{1,0:T(8,128)(2,1)}, bf16[512,256]{1,0:T(8,128)(2,1)}, u32[]{:S(2)}, u32[]{:S(2)}) collective-permute-start(bf16[512,256]{1,0:T(8,128)(2,1)} %get-tuple-element.17), channel_id=1, source_target_pairs={{0,4},{4,8},{8,12},{12,16},{16,20},{20,24},{24,28},{28,0},{1,5},{5... | collective-permute-start | bytes 786440 | tf_op jit(solution)/shard_map/ppermute | solution.py:20
  452.3 25.3 %collective-permute-start.1 = (bf16[512,256]{1,0:T(8,128)(2,1)}, bf16[512,256]{1,0:T(8,128)(2,1)}, u32[]{:S(2)}, u32[]{:S(2)}) collective-permute-start(bf16[512,256]{1,0:T(8,128)(2,1)} %get-tuple-element.17), channel_id=1, source_target_pairs={{0,28},{4,0},{8,4},{12,8},{16,12},{20,16},{24,20},{28,24},{1,29},{... | collective-permute-start | bytes 786440 | tf_op jit(solution)/shard_map/ppermute | solution.py:25
  467.1 1.6 copy-start.5
  469.5 6.2 %copy-start.16 = (f32[2,1024]{1,0:T(2,128)S(1)}, f32[2,1024]{1,0:T(2,128)}, u32[]{:S(2)}) copy-start(f32[2,1024]{1,0:T(2,128)} %param.27) | copy-start | bytes 24580
  469.6 11.6 %copy-start.3 = (f32[1024,704]{0,1:T(8,128)S(1)}, f32[1024,704]{0,1:T(8,128)}, u32[]{:S(2)}) copy-start(f32[1024,704]{0,1:T(8,128)} %copy-done.2) | copy-start | bytes 8650756
  469.6 11.5 %copy-start.6 = (f32[1024,704]{0,1:T(8,128)S(1)}, f32[1024,704]{0,1:T(8,128)}, u32[]{:S(2)}) copy-start(f32[1024,704]{0,1:T(8,128)} %copy-done.5) | copy-start | bytes 8650756
  476.4 14.4 %collective-permute-start.2 = (bf16[512,256]{1,0:T(8,128)(2,1)}, bf16[512,256]{1,0:T(8,128)(2,1)S(1)}, u32[]{:S(2)}, u32[]{:S(2)}) collective-permute-start(bf16[512,256]{1,0:T(8,128)(2,1)} %collective-permute-done), channel_id=1, source_target_pairs={{0,4},{4,8},{8,12},{12,16},{16,20},{20,24},{24,28},{28,0},{1,5},{5... | collective-permute-start | bytes 786440 | tf_op jit(solution)/shard_map/ppermute | solution.py:20
  477.6 18.9 %collective-permute-start.3 = (bf16[512,256]{1,0:T(8,128)(2,1)}, bf16[512,256]{1,0:T(8,128)(2,1)S(1)}, u32[]{:S(2)}, u32[]{:S(2)}) collective-permute-start(bf16[512,256]{1,0:T(8,128)(2,1)} %collective-permute-done.1), channel_id=1, source_target_pairs={{0,28},{4,0},{8,4},{12,8},{16,12},{20,16},{24,20},{28,24},{1,29},{... | collective-permute-start | bytes 786440 | tf_op jit(solution)/shard_map/ppermute | solution.py:25
  490.8 14.0 %collective-permute-start.4 = (bf16[512,256]{1,0:T(8,128)(2,1)S(1)}, bf16[512,256]{1,0:T(8,128)(2,1)S(1)}, u32[]{:S(2)}, u32[]{:S(2)}) collective-permute-start(bf16[512,256]{1,0:T(8,128)(2,1)S(1)} %collective-permute-done.2), channel_id=1, source_target_pairs={{0,4},{4,8},{8,12},{12,16},{16,20},{20,24},{24,28},{28,0},{1,5},{5... | collective-permute-start | bytes 786440 | tf_op jit(solution)/shard_map/ppermute | solution.py:20
  496.5 12.2 %collective-permute-start.5 = (bf16[512,256]{1,0:T(8,128)(2,1)S(1)}, bf16[512,256]{1,0:T(8,128)(2,1)S(1)}, u32[]{:S(2)}, u32[]{:S(2)}) collective-permute-start(bf16[512,256]{1,0:T(8,128)(2,1)S(1)} %collective-permute-done.3), channel_id=1, source_target_pairs={{0,28},{4,0},{8,4},{12,8},{16,12},{20,16},{24,20},{28,24},{1,29},{... | collective-permute-start | bytes 786440 | tf_op jit(solution)/shard_map/ppermute | solution.py:25
  504.7 9.2 %collective-permute-start.6 = (bf16[512,256]{1,0:T(8,128)(2,1)S(1)}, bf16[512,256]{1,0:T(8,128)(2,1)S(1)}, u32[]{:S(2)}, u32[]{:S(2)}) collective-permute-start(bf16[512,256]{1,0:T(8,128)(2,1)S(1)} %collective-permute-done.4), channel_id=1, source_target_pairs={{0,4},{4,8},{8,12},{12,16},{16,20},{20,24},{24,28},{28,0},{1,5},{5... | collective-permute-start | bytes 786440 | tf_op jit(solution)/shard_map/ppermute | solution.py:20
Sparse Core Ops, SparseCore 0:
  36.0 132.6 all-reduce.13
  178.0 70.6 all-reduce.7
  254.7 129.2 all-reduce.11
  392.6 71.0 all-reduce.9
  469.7 58.8 all-gather.1
